TPU v7x, 256 devices: a whole 4x4x8 slice. The times are simulated.
256 devices in a mesh: space: 32 (over z_hi, x, core), scen: 8 (over y, z_lo).
Axes of the slice: x: 4, y: 4, z: 8 (z_hi: 4, z_lo: 2; z = z_hi * 2 + z_lo), core: 2. Of those that a mesh axis runs over, the one named last changes fastest.
Arguments:
- concentration: float32 [8, 8, 6, 384, 384], P('scen', None, None, 'space'), may hold values from -6 to 6
- emissions: float32 [8, 6, 384, 384], P('scen', None, 'space'), may hold values from -3 to 3
- courant: float32 [2, 8, 6, 384, 384], P(None, None, None, 'space'), may hold values from -0.9 to 0.9
- tile_source: int32 [8640], P('space'), may hold values from 0 to 215, as said below
- tile_target: int32 [8640], P('space'), may hold values from 0 to 1023, as said below
- intersection: bfloat16 [8640, 128, 128], P('space'), may hold values from 0 to 0.0625
Outputs:
- transported: float32 [8, 8, 6, 384, 384], P('scen', None, None, 'space')
- regridded: float32 [8, 8, 1024, 128], P('scen', None, 'space')
- ensemble_moments: float32 [2, 8, 1024, 128], P(None, None, 'space')
Inputs may be any that keep to these rules, and one draw needn't show every extreme that they name: `tile_source`: every source block of a row band is named by at least one of the band's tiles. `tile_target`: latitude band b holds target blocks b * 32 to (b+1) * 32 - 1. The 270 tiles of one row band name at most 16 blocks of any one latitude band and at least 8 of every latitude band but one, which receives exactly 16 tiles from every row band. Every target block is named by some tile.
All inputs are finite; a program needn't handle non-finite values.
Results may differ from a plain program's by a relative error of at most 0.0027.
Values sent between devices are 32-bit elements; how exact they have to be, the bound alone decides.
No kernel may reach another device: no remote copies, remote signals or barrier semaphores. Data moves between devices by JAX's collectives and lax.ppermute only.
A program may use at most 128 MiB of HBM per device.

v0:
```python
import jax
import jax.numpy as jnp
from jax import lax
from jax.sharding import PartitionSpec as P

TGT_DEV = 32


def broadcast(value, axis, source):
    kept = jnp.where(lax.axis_index(axis) == source, value, 0).astype(value.dtype)
    return lax.psum(kept, axis)


def from_behind(block, axis, distance):
    devices = range(lax.axis_size(axis))
    route = [((i - distance) % len(devices), i) for i in devices]
    return lax.ppermute(block, axis, route)


def parabola_sweep(padded, courant_faces, sweep_axis):
    cells_along = padded.shape[sweep_axis] - 6

    def window(values_in, first_cell, length):
        return lax.slice_in_dim(values_in, first_cell, first_cell + length, axis=sweep_axis)

    edge_values = 7.0 / 12.0 * (
        window(padded, 1, cells_along + 3) + window(padded, 2, cells_along + 3)
    ) - 1.0 / 12.0 * (window(padded, 0, cells_along + 3) + window(padded, 3, cells_along + 3))
    left_edge = window(edge_values, 0, cells_along + 2)
    right_edge = window(edge_values, 1, cells_along + 2)
    centre = window(padded, 2, cells_along + 2)
    slopes = right_edge - left_edge
    curvature = 6.0 * centre - 3.0 * (left_edge + right_edge)
    backward = -courant_faces
    upwind_left = courant_faces * (
        window(right_edge, 0, cells_along + 1)
        - 0.5
        * courant_faces
        * (
            window(slopes, 0, cells_along + 1)
            - (1.0 - 2.0 * courant_faces / 3.0) * window(curvature, 0, cells_along + 1)
        )
    )
    upwind_right = courant_faces * (
        window(left_edge, 1, cells_along + 1)
        + 0.5
        * backward
        * (
            window(slopes, 1, cells_along + 1)
            + (1.0 - 2.0 * backward / 3.0) * window(curvature, 1, cells_along + 1)
        )
    )
    fluxes = jnp.where(courant_faces >= 0.0, upwind_left, upwind_right)
    return window(padded, 3, cells_along) - (
        window(fluxes, 1, cells_along) - window(fluxes, 0, cells_along)
    )


def pack_rows(tracer, north_wind, lowest):
    row_count = tracer.shape[3]
    width_cells = tracer.shape[4]
    if lowest:
        layers = tracer[:, :, :, 0:3, :]
        wind_row = north_wind[:, :, 0:1, :]
    else:
        layers = tracer[:, :, :, row_count - 3 :, :]
        wind_row = north_wind[:, :, row_count - 1 :, :]
    return jnp.concatenate([layers.reshape(-1, width_cells), wind_row.reshape(-1, width_cells)], 0)


def unpack_rows(packed, tracer_shape):
    split_at = tracer_shape[0] * tracer_shape[1] * 18
    layers = packed[:split_at].reshape(tracer_shape[0], tracer_shape[1], 6, 3, packed.shape[1])
    wind_row = packed[split_at:].reshape(tracer_shape[1], 6, packed.shape[1])
    return (layers, wind_row)


def column_halos(tracer, east_wind, north_wind, position, band_count):
    row_count = tracer.shape[3]
    width_cells = tracer.shape[4]
    received = []
    for root_rank, lowest in ((band_count - 1, False), (0, True)):
        packed = pack_rows(tracer, north_wind, lowest)
        received.append(unpack_rows(broadcast(packed, "space", root_rank), tracer.shape))
    top_layers, top_wind = received[0]
    low_layers, low_wind = received[1]
    start_column = width_cells - (position + 1) * row_count
    padded_faces = []
    speed_faces = []
    for face_number in range(6):
        if face_number % 2 == 0:
            source = lax.dynamic_slice_in_dim(
                top_layers[:, :, (face_number - 2) % 6], start_column, row_count, axis=3
            )
            west_cells = jnp.swapaxes(jnp.flip(source, -1), -1, -2)
            west_speed = jnp.flip(
                lax.dynamic_slice_in_dim(
                    top_wind[:, (face_number - 2) % 6], start_column, row_count, axis=1
                ),
                -1,
            )
            east_cells = tracer[:, :, (face_number + 1) % 6, :, 0:3]
            east_speed = east_wind[:, (face_number + 1) % 6, :, 0]
        else:
            west_cells = tracer[:, :, (face_number - 1) % 6, :, width_cells - 3 :]
            west_speed = east_wind[:, (face_number - 1) % 6, :, width_cells - 1]
            source = lax.dynamic_slice_in_dim(
                low_layers[:, :, (face_number + 2) % 6], start_column, row_count, axis=3
            )
            east_cells = jnp.swapaxes(jnp.flip(source, -1), -1, -2)
            east_speed = jnp.flip(
                lax.dynamic_slice_in_dim(
                    low_wind[:, (face_number + 2) % 6], start_column, row_count, axis=1
                ),
                -1,
            )
        padded_faces.append(
            jnp.concatenate([west_cells, tracer[:, :, face_number], east_cells], -1)
        )
        speeds = jnp.concatenate(
            [west_speed[:, :, None], east_wind[:, face_number], east_speed[:, :, None]], -1
        )
        speed_faces.append(0.5 * (speeds[:, :, :-1] + speeds[:, :, 1:]))
    return (jnp.stack(padded_faces, 2), jnp.stack(speed_faces, 1))


def row_halos(tracer, east_wind, north_wind, position, band_count):
    scenarios = tracer.shape[0]
    levels = tracer.shape[1]
    row_count = tracer.shape[3]
    width_cells = tracer.shape[4]
    shifted = []
    for step_by, lowest in ((-1, True), (1, False)):
        packed = pack_rows(tracer, north_wind, lowest)
        shifted.append(unpack_rows(from_behind(packed, "space", step_by), tracer.shape))
    above_layers, above_wind = shifted[0]
    below_layers, below_wind = shifted[1]
    columns = jnp.concatenate([tracer[..., 0:3], tracer[..., width_cells - 3 :]], -1)
    columns = jnp.swapaxes(columns, -1, -2).reshape(-1, row_count)
    column_speed = jnp.stack([east_wind[..., 0], east_wind[..., width_cells - 1]], -2).reshape(
        -1, row_count
    )
    gathered = lax.all_gather(
        jnp.concatenate([columns, column_speed], 0), "space", axis=1, tiled=True
    )
    split_at = scenarios * levels * 36
    edge_layers = gathered[:split_at].reshape(scenarios, levels, 6, 6, -1)
    edge_speed = gathered[split_at:].reshape(levels, 6, 2, -1)
    at_top = position == band_count - 1
    at_bottom = position == 0
    padded_faces = []
    speed_faces = []
    for face_number in range(6):
        if face_number % 2 == 0:
            north_cells = jnp.where(
                at_top,
                jnp.flip(edge_layers[:, :, (face_number + 2) % 6, 0:3], -1),
                above_layers[:, :, face_number],
            )
            north_speed = jnp.where(
                at_top,
                jnp.flip(edge_speed[:, (face_number + 2) % 6, 0], -1),
                above_wind[:, face_number],
            )
            south_cells = jnp.where(
                at_bottom,
                below_layers[:, :, (face_number - 1) % 6],
                below_layers[:, :, face_number],
            )
            south_speed = jnp.where(
                at_bottom, below_wind[:, (face_number - 1) % 6], below_wind[:, face_number]
            )
        else:
            north_cells = jnp.where(
                at_top, above_layers[:, :, (face_number + 1) % 6], above_layers[:, :, face_number]
            )
            north_speed = jnp.where(
                at_top, above_wind[:, (face_number + 1) % 6], above_wind[:, face_number]
            )
            south_cells = jnp.where(
                at_bottom,
                jnp.flip(edge_layers[:, :, (face_number - 2) % 6, 3:6], -1),
                below_layers[:, :, face_number],
            )
            south_speed = jnp.where(
                at_bottom,
                jnp.flip(edge_speed[:, (face_number - 2) % 6, 1], -1),
                below_wind[:, face_number],
            )
        padded_faces.append(
            jnp.concatenate([south_cells, tracer[:, :, face_number], north_cells], -2)
        )
        speeds = jnp.concatenate(
            [south_speed[:, None, :], north_wind[:, face_number], north_speed[:, None, :]], -2
        )
        speed_faces.append(0.5 * (speeds[:, :-1, :] + speeds[:, 1:, :]))
    return (jnp.stack(padded_faces, 2), jnp.stack(speed_faces, 1))


def local(concentration, emissions, courant, tile_source, tile_target, intersection):
    band_count = lax.axis_size("space")
    position = lax.axis_index("space")
    tracer = concentration.at[:, 0].add(emissions)
    east_wind = courant[0]
    north_wind = courant[1]
    for step_number in range(2):
        padded, courant_faces = column_halos(tracer, east_wind, north_wind, position, band_count)
        tracer = parabola_sweep(padded, courant_faces, 4)
        padded, courant_faces = row_halos(tracer, east_wind, north_wind, position, band_count)
        tracer = parabola_sweep(padded, courant_faces, 3)
    scenarios = tracer.shape[0]
    levels = tracer.shape[1]
    batch_rows = scenarios * levels
    block_cells = intersection.shape[1]
    blocks = tracer.astype(jnp.bfloat16).reshape(batch_rows, -1, block_cells)
    chosen = jnp.take(blocks, tile_source, axis=1)
    partial_value = jnp.einsum(
        "btk,tkc->tbc", chosen, intersection, preferred_element_type=jnp.float32
    )
    inside = (tile_target >= 0) & (tile_target < TGT_DEV * lax.axis_size("space"))
    slot_index = jnp.where(inside, tile_target, TGT_DEV * lax.axis_size("space"))
    empty = jnp.zeros((TGT_DEV * lax.axis_size("space"), batch_rows, block_cells), jnp.float32)
    summed = lax.psum_scatter(
        empty.at[slot_index].add(partial_value, mode="drop"),
        "space",
        scatter_dimension=0,
        tiled=True,
    )
    band_result = jnp.swapaxes(summed, 0, 1)
    regridded = band_result.reshape(scenarios, levels, TGT_DEV, block_cells)
    moment_sums = jnp.stack([jnp.sum(regridded, 0), jnp.sum(regridded * regridded, 0)])
    summed_moments = lax.psum(moment_sums, "scen")
    ensemble_moments = summed_moments / (scenarios * lax.axis_size("scen"))
    return (tracer, regridded, ensemble_moments)


def solution(mesh):
    return jax.shard_map(
        local,
        mesh=mesh,
        in_specs=(
            P("scen", None, None, "space", None),
            P("scen", None, "space", None),
            P(None, None, None, "space", None),
            P("space"),
            P("space"),
            P("space", None, None),
        ),
        out_specs=(
            P("scen", None, None, "space", None),
            P("scen", None, "space", None),
            P(None, None, "space", None),
        ),
        check_vma=False,
    )
```

profile of v0, /device:TPU:2, one launch (start us, length us, event | category | flops | bytes accessed | tf_op | source)
XLA Modules:
  0.0 1000.3 jit_solution(16481117192037455923)
XLA Ops:
  8.4 1.6 slice_bitcast_fusion
  12.5 1.7 fusion.60
  15.7 5.9 copy.2796
  21.6 7.1 fusion.179
  31.4 1.9 copy.2633
  34.1 2.6 copy.2637
  36.7 1.4 copy.2636
  38.1 2.6 copy.2641
  41.5 2.6 copy.2645
  44.8 2.6 copy.2649
  53.0 240.5 %all-reduce.10.cloned.1.call-done = (f32[192,384]{1,0:T(8,128)}, f32[192,384]{1,0:T(8,128)}) async-done(((f32[192,384]{1,0:T(8,128)}, f32[192,384]{1,0:T(8,128)}), (f32[192,384]{1,0:T(8,128)}, f32[192,384]{1,0:T(8,128)})) %all-reduce.10.cloned.1.call-update) | async-done | bytes 589840 | tf_op jit(solution)/shard_map/psum | solution.py:11
  296.3 1.5 slice.1216
  304.3 1.7 slice_subtract_fusion.1
  306.0 1.5 reshape.5219
  307.6 1.7 fusion.199
  316.5 1.9 bitcast_dynamic-update-slice_fusion.10
  318.4 1.8 constant_dynamic-update-slice_fusion.4
  320.2 1.8 bitcast_dynamic-update-slice_fusion.9
  327.7 2.7 fusion.17
  333.5 45.6 %all-gather = f32[32,12,384]{2,1,0:T(8,128)S(1)} all-gather(f32[1,12,384]{2,1,0:T(8,128)S(1)} %fusion.150), channel_id=1, replica_groups=mesh['space'=32,'scen'=8] {'space'}, dimensions={0}, use_global_device_ids=true | all-gather | bytes 608256 | tf_op jit(solution)/shard_map/all_gather | solution.py:143
  380.7 2.7 collective-permute-start.1
  407.0 275.7 %all-reduce.8.cloned.1.call-done = (f32[192,384]{1,0:T(8,128)}, f32[192,384]{1,0:T(8,128)}) async-done(((f32[192,384]{1,0:T(8,128)}, f32[192,384]{1,0:T(8,128)}), (f32[192,384]{1,0:T(8,128)}, f32[192,384]{1,0:T(8,128)})) %all-reduce.8.cloned.1.call-update) | async-done | bytes 589840 | tf_op jit(solution)/shard_map/psum | solution.py:11
  706.2 45.6 %all-gather.1 = f32[32,12,384]{2,1,0:T(8,128)S(1)} all-gather(f32[1,12,384]{2,1,0:T(8,128)S(1)} %fusion.151), channel_id=1, replica_groups=mesh['space'=32,'scen'=8] {'space'}, dimensions={0}, use_global_device_ids=true | all-gather | bytes 608256 | tf_op jit(solution)/shard_map/all_gather | solution.py:143
  753.1 2.6 collective-permute-start.3
  775.8 1.8 gather_fusion
  777.6 4.9 fusion.56
  782.5 2.3 broadcast_in_dim.40
  784.8 27.1 %scatter_fusion = f32[1024,8,128]{2,1,0:T(8,128)} fusion(f32[1024,8,128]{2,1,0:T(8,128)} %broadcast_in_dim.40, s32[270]{0:T(512)S(1)} %copy-done.76, f32[270,8,128]{2,1,0:T(8,128)S(1)} %fusion.56), kind=kCustom, calls=%fused_computation.1 | custom fusion | flops 276480 | bytes 3318840 | tf_op jit(solution)/shard_map/scatter-add | solution.py:224
  812.0 99.2 %reduce-scatter.2.cloned.1.call-done = f32[32,8,128]{2,1,0:T(8,128)} async-done(((f32[1024,8,128]{2,1,0:T(8,128)}), f32[32,8,128]{2,1,0:T(8,128)}) %reduce-scatter.2.cloned.1.call-update) | async-done | bytes 131088 | tf_op jit(solution)/shard_map/reduce_scatter | solution.py:223
  912.1 1.6 pad_maximum_fusion.8
  913.7 1.6 copy.2791
  915.3 76.7 %all-reduce.6.cloned.1.call-done = f32[2,8,32,128]{3,1,2,0:T(8,128)} async-done(((f32[2,8,32,128]{3,1,2,0:T(8,128)}), f32[2,8,32,128]{3,1,2,0:T(8,128)}) %all-reduce.6.cloned.1.call-update) | async-done | bytes 262160 | tf_op jit(solution)/shard_map/psum | solution.py:232
  (550 shorter events, 112.2 us)
Async XLA Ops:
  7.2 286.3 %all-reduce.10.cloned.1.call-start = ((), (), s32[]{:S(2)}) async-start(), calls=%async_computation.4 | async-start | bytes 1179648 | tf_op jit(solution)/shard_map/psum | solution.py:11
  14.9 667.8 %all-reduce.8.cloned.1.call-start = ((), (), s32[]{:S(2)}) async-start(), calls=%async_computation.3 | async-start | bytes 1179648 | tf_op jit(solution)/shard_map/psum | solution.py:11
  33.3 266.2 %copy-start.10 = (f32[8,1,12,384]{3,0,2,1:T(8,128)}, f32[8,1,12,384]{3,0,2,1:T(8,128)S(1)}, u32[]{:S(2)}) copy-start(f32[8,1,12,384]{3,0,2,1:T(8,128)S(1)} %copy.2633) | copy-start | bytes 442372
  34.1 265.4 %copy-start.35 = (f32[8,1,12,1]{3,0,2,1:T(8,128)}, f32[8,1,12,1]{3,0,2,1:T(8,128)S(1)}, u32[]{:S(2)}) copy-start(f32[8,1,12,1]{3,0,2,1:T(8,128)S(1)} %copy.2635) | copy-start | bytes 1156
  51.9 281.4 %copy-start.69 = (f32[96,12]{0,1:T(8,128)}, f32[96,12]{0,1:T(8,128)S(1)}, u32[]{:S(2)}) copy-start(f32[96,12]{0,1:T(8,128)S(1)} %copy.2662) | copy-start | bytes 13828
  316.5 5.5 copy-start.7
  316.5 5.5 copy-start.32
  316.5 5.5 copy-start.40
  316.5 6.4 copy-start.5
  316.5 6.4 copy-start.30
  316.5 6.4 copy-start.41
  318.4 6.1 copy-start.3
  318.4 6.1 copy-start.28
  318.4 6.1 copy-start.42
  322.0 4.0 copy-start.1
  322.0 4.0 copy-start.26
  322.0 4.0 copy-start.43
  332.7 59.0 %collective-permute-start = (f32[192,384]{1,0:T(8,128)}, f32[192,384]{1,0:T(8,128)}, u32[]{:S(2)}, u32[]{:S(2)}) collective-permute-start(f32[192,384]{1,0:T(8,128)} %pad_maximum_fusion.2), channel_id=1, source_target_pairs={{248,0},{0,8},{8,16},{16,24},{24,32},{32,40},{40,48},{48,56},{56,6... | collective-permute-start | bytes 884744 | tf_op jit(solution)/shard_map/ppermute | solution.py:17
  380.7 12.1 %collective-permute-start.1 = (f32[192,384]{1,0:T(8,128)}, f32[192,384]{1,0:T(8,128)S(1)}, u32[]{:S(2)}, u32[]{:S(2)}) collective-permute-start(f32[192,384]{1,0:T(8,128)} %pad_maximum_fusion.6), channel_id=1, source_target_pairs={{8,0},{16,8},{24,16},{32,24},{40,32},{48,40},{56,48},{64,56},{72,6... | collective-permute-start | bytes 884744 | tf_op jit(solution)/shard_map/ppermute | solution.py:17
  383.9 9.5 copy-start.17
  406.1 505.1 %reduce-scatter.2.cloned.1.call-start = ((), (), s32[]{:S(2)}) async-start(), calls=%async_computation.1 | async-start | bytes 4325376 | tf_op jit(solution)/shard_map/reduce_scatter | solution.py:223
  406.9 277.1 %copy-start.11 = (f32[8,1,12,384]{3,0,2,1:T(8,128)S(1)}, f32[8,1,12,384]{3,0,2,1:T(8,128)}, u32[]{:S(2)}) copy-start(f32[8,1,12,384]{3,0,2,1:T(8,128)} %copy-done.10) | copy-start | bytes 442372
  406.9 277.1 %copy-start.36 = (f32[8,1,12,1]{3,0,2,1:T(8,128)S(1)}, f32[8,1,12,1]{3,0,2,1:T(8,128)}, u32[]{:S(2)}) copy-start(f32[8,1,12,1]{3,0,2,1:T(8,128)} %copy-done.35) | copy-start | bytes 1156
  684.0 4.2 copy-start.9
  684.0 4.2 copy-start.34
  685.6 4.2 copy-start.8
  685.6 4.2 copy-start.33
  686.7 4.8 copy-start.6
  686.7 4.8 copy-start.31
  705.4 61.8 %collective-permute-start.2 = (f32[192,384]{1,0:T(8,128)}, f32[192,384]{1,0:T(8,128)}, u32[]{:S(2)}, u32[]{:S(2)}) collective-permute-start(f32[192,384]{1,0:T(8,128)} %pad_maximum_fusion), channel_id=1, source_target_pairs={{248,0},{0,8},{8,16},{16,24},{24,32},{32,40},{40,48},{48,56},{56,6... | collective-permute-start | bytes 884744 | tf_op jit(solution)/shard_map/ppermute | solution.py:17
  753.1 15.6 %collective-permute-start.3 = (f32[192,384]{1,0:T(8,128)}, f32[192,384]{1,0:T(8,128)S(1)}, u32[]{:S(2)}, u32[]{:S(2)}) collective-permute-start(f32[192,384]{1,0:T(8,128)} %pad_maximum_fusion.4), channel_id=1, source_target_pairs={{8,0},{16,8},{24,16},{32,24},{40,32},{48,40},{56,48},{64,56},{72,6... | collective-permute-start | bytes 884744 | tf_op jit(solution)/shard_map/ppermute | solution.py:17
  811.9 180.1 %all-reduce.6.cloned.1.call-start = ((), (), s32[]{:S(2)}) async-start(), calls=%async_computation.2 | async-start | bytes 524288 | tf_op jit(solution)/shard_map/psum | solution.py:232
  (55 other events, 100.5 us)
Sparse Core Ops, SparseCore 0:
  15.0 278.3 all-reduce.9
  406.2 276.4 all-reduce.7
  812.0 99.0 reduce-scatter.1
  914.2 77.8 all-reduce.5
where the time goes:
time: 1000 us
  waiting for transfers between devices  692 us (69%)
  local copies, waits for them, and re-layouts  112 us (11%)
  blocking collectives  91.1 us (9%)
  other arithmetic  78.5 us (8%)
  between operations  15.8 us (2%)
    psum x2, waiting for transfers between devices, broadcast(): return lax.psum(kept, axis)  516 us
    reduce_scatter x1, waiting for transfers between devices, local(): lax.psum_scatter(empty.at[slot_index].add(partial_value, mode='drop'), 's...  99.2 us
    all_gather x2, blocking collectives, row_halos(): lax.all_gather(jnp.concatenate([columns, column_speed], 0), 'space', axis...  91.1 us
    psum x1, waiting for transfers between devices, local(): summed_moments = lax.psum(moment_sums, 'scen')  76.7 us
    scatter-add x1, other arithmetic, local(): empty.at[slot_index].add(partial_value, mode='drop')  27.1 us
    unnamed x62, other arithmetic  21.1 us
    slice x7, local copies, waits for them, and re-layouts, column_halos(): east_wind[:, face_number]  20.5 us
  transfers between devices with their start and end apart: 8, of which 4 were waited for; matrix products, arithmetic and copies ran while one was open for 7% of the time, Pallas kernels for 0%

commit v1 on v0

v1 whole, which is shorter than its diff:
```python
import jax
import jax.numpy as jnp
from jax import lax
from jax.sharding import PartitionSpec as P

TGT_DEV = 32
SLOTS = 16


def from_behind(block, axis, distance):
    devices = range(lax.axis_size(axis))
    route = [((i - distance) % len(devices), i) for i in devices]
    return lax.ppermute(block, axis, route)


def parabola_sweep(padded, courant_faces, sweep_axis):
    cells_along = padded.shape[sweep_axis] - 6

    def window(values_in, first_cell, length):
        return lax.slice_in_dim(values_in, first_cell, first_cell + length, axis=sweep_axis)

    edge_values = 7.0 / 12.0 * (
        window(padded, 1, cells_along + 3) + window(padded, 2, cells_along + 3)
    ) - 1.0 / 12.0 * (window(padded, 0, cells_along + 3) + window(padded, 3, cells_along + 3))
    left_edge = window(edge_values, 0, cells_along + 2)
    right_edge = window(edge_values, 1, cells_along + 2)
    centre = window(padded, 2, cells_along + 2)
    slopes = right_edge - left_edge
    curvature = 6.0 * centre - 3.0 * (left_edge + right_edge)
    backward = -courant_faces
    upwind_left = courant_faces * (
        window(right_edge, 0, cells_along + 1)
        - 0.5
        * courant_faces
        * (
            window(slopes, 0, cells_along + 1)
            - (1.0 - 2.0 * courant_faces / 3.0) * window(curvature, 0, cells_along + 1)
        )
    )
    upwind_right = courant_faces * (
        window(left_edge, 1, cells_along + 1)
        + 0.5
        * backward
        * (
            window(slopes, 1, cells_along + 1)
            + (1.0 - 2.0 * backward / 3.0) * window(curvature, 1, cells_along + 1)
        )
    )
    fluxes = jnp.where(courant_faces >= 0.0, upwind_left, upwind_right)
    return window(padded, 3, cells_along) - (
        window(fluxes, 1, cells_along) - window(fluxes, 0, cells_along)
    )


def by_destination(values, band_count):
    width = values.shape[-1]
    blocks = values.reshape(values.shape[:-1] + (band_count, width // band_count))
    return jnp.flip(jnp.moveaxis(blocks, -2, 0), 0).reshape(band_count, -1)


def pack_rows(tracer, north_wind, lowest):
    row_count = tracer.shape[3]
    width_cells = tracer.shape[4]
    if lowest:
        layers = tracer[:, :, :, 0:3, :]
    else:
        layers = tracer[:, :, :, row_count - 3 :, :]
    parts = [layers.reshape(-1, width_cells)]
    if north_wind is not None:
        wind_row = north_wind[:, :, 0:1, :] if lowest else north_wind[:, :, row_count - 1 :, :]
        parts.append(wind_row.reshape(-1, width_cells))
    return jnp.concatenate(parts, 0)


def edge_rows(tracer, north_wind, position, band_count, with_wind):
    row_count = tracer.shape[3]
    top_parts = [by_destination(tracer[:, :, 0::2, row_count - 3 :, :], band_count)]
    low_parts = [by_destination(tracer[:, :, 1::2, 0:3, :], band_count)]
    if with_wind:
        top_parts.append(by_destination(north_wind[:, 0::2, row_count - 1, :], band_count))
        low_parts.append(by_destination(north_wind[:, 1::2, 0, :], band_count))
    send_top = jnp.concatenate(top_parts, 1)
    send_low = jnp.concatenate(low_parts, 1)
    send = jnp.where(
        position == band_count - 1, send_top, jnp.where(position == 0, send_low, 0.0)
    ).astype(send_top.dtype)
    got = lax.all_to_all(send, "space", 0, 0, tiled=True)
    return got[band_count - 1], got[0]


def column_halos(tracer, east_wind, north_wind, position, band_count, edge_wind):
    scenarios, levels, _, row_count, width_cells = tracer.shape
    top, low = edge_rows(tracer, north_wind, position, band_count, edge_wind is None)
    cells = scenarios * levels * 3 * 3 * row_count
    top_layers = top[:cells].reshape(scenarios, levels, 3, 3, row_count)
    low_layers = low[:cells].reshape(scenarios, levels, 3, 3, row_count)
    if edge_wind is None:
        edge_wind = (
            top[cells:].reshape(levels, 3, row_count),
            low[cells:].reshape(levels, 3, row_count),
        )
    top_wind, low_wind = edge_wind
    padded_faces = []
    speed_faces = []
    for face_number in range(6):
        half = face_number // 2
        if face_number % 2 == 0:
            source = top_layers[:, :, (half - 1) % 3]
            west_cells = jnp.swapaxes(jnp.flip(source, -1), -1, -2)
            west_speed = jnp.flip(top_wind[:, (half - 1) % 3], -1)
            east_cells = tracer[:, :, (face_number + 1) % 6, :, 0:3]
            east_speed = east_wind[:, (face_number + 1) % 6, :, 0]
        else:
            west_cells = tracer[:, :, (face_number - 1) % 6, :, width_cells - 3 :]
            west_speed = east_wind[:, (face_number - 1) % 6, :, width_cells - 1]
            source = low_layers[:, :, (half + 1) % 3]
            east_cells = jnp.swapaxes(jnp.flip(source, -1), -1, -2)
            east_speed = jnp.flip(low_wind[:, (half + 1) % 3], -1)
        padded_faces.append(
            jnp.concatenate([west_cells, tracer[:, :, face_number], east_cells], -1)
        )
        speeds = jnp.concatenate(
            [west_speed[:, :, None], east_wind[:, face_number], east_speed[:, :, None]], -1
        )
        speed_faces.append(0.5 * (speeds[:, :, :-1] + speeds[:, :, 1:]))
    return (jnp.stack(padded_faces, 2), jnp.stack(speed_faces, 1), edge_wind)


def edge_columns(tracer, east_wind, position, band_count, with_wind):
    scenarios, levels, _, row_count, width_cells = tracer.shape
    to_top = [jnp.swapaxes(tracer[:, :, 0::2, :, 0:3], -1, -2).reshape(-1)]
    to_low = [jnp.swapaxes(tracer[:, :, 1::2, :, width_cells - 3 :], -1, -2).reshape(-1)]
    if with_wind:
        to_top.append(east_wind[:, 0::2, :, 0].reshape(-1))
        to_low.append(east_wind[:, 1::2, :, width_cells - 1].reshape(-1))
    to_top = jnp.concatenate(to_top)
    to_low = jnp.concatenate(to_low)
    send = jnp.zeros((band_count,) + to_top.shape, to_top.dtype)
    send = send.at[band_count - 1].set(to_top).at[0].set(to_low)
    got = lax.all_to_all(send, "space", 0, 0, tiled=True)
    cells = scenarios * levels * 3 * 3 * row_count
    layers = got[:, :cells].reshape(band_count, scenarios, levels, 3, 3, row_count)
    layers = jnp.moveaxis(layers, 0, -2).reshape(scenarios, levels, 3, 3, band_count * row_count)
    wind = None
    if with_wind:
        wind = got[:, cells:].reshape(band_count, levels, 3, row_count)
        wind = jnp.moveaxis(wind, 0, -2).reshape(levels, 3, band_count * row_count)
    return layers, wind


def row_halos(tracer, east_wind, north_wind, position, band_count, row_wind):
    first_step = row_wind is None
    shifted = []
    for step_by, lowest in ((-1, True), (1, False)):
        packed = pack_rows(tracer, north_wind if first_step else None, lowest)
        shifted.append(from_behind(packed, "space", step_by))
    edge_layers, edge_speed = edge_columns(tracer, east_wind, position, band_count, first_step)
    layer_rows = tracer.shape[0] * tracer.shape[1] * 18
    width_cells = tracer.shape[4]
    if first_step:
        levels = tracer.shape[1]
        row_wind = tuple(
            packed[layer_rows:].reshape(levels, 6, width_cells) for packed in shifted
        ) + (edge_speed,)
    above_wind, below_wind, edge_speed = row_wind
    above_layers, below_layers = (
        packed[:layer_rows].reshape(tracer.shape[0], tracer.shape[1], 6, 3, width_cells)
        for packed in shifted
    )
    at_top = position == band_count - 1
    at_bottom = position == 0
    padded_faces = []
    speed_faces = []
    for face_number in range(6):
        half = face_number // 2
        if face_number % 2 == 0:
            north_cells = jnp.where(
                at_top,
                jnp.flip(edge_layers[:, :, (half + 1) % 3], -1),
                above_layers[:, :, face_number],
            )
            north_speed = jnp.where(
                at_top,
                jnp.flip(edge_speed[:, (half + 1) % 3], -1),
                above_wind[:, face_number],
            )
            south_cells = jnp.where(
                at_bottom,
                below_layers[:, :, (face_number - 1) % 6],
                below_layers[:, :, face_number],
            )
            south_speed = jnp.where(
                at_bottom, below_wind[:, (face_number - 1) % 6], below_wind[:, face_number]
            )
        else:
            north_cells = jnp.where(
                at_top, above_layers[:, :, (face_number + 1) % 6], above_layers[:, :, face_number]
            )
            north_speed = jnp.where(
                at_top, above_wind[:, (face_number + 1) % 6], above_wind[:, face_number]
            )
            south_cells = jnp.where(
                at_bottom,
                jnp.flip(edge_layers[:, :, (half - 1) % 3], -1),
                below_layers[:, :, face_number],
            )
            south_speed = jnp.where(
                at_bottom,
                jnp.flip(edge_speed[:, (half - 1) % 3], -1),
                below_wind[:, face_number],
            )
        padded_faces.append(
            jnp.concatenate([south_cells, tracer[:, :, face_number], north_cells], -2)
        )
        speeds = jnp.concatenate(
            [south_speed[:, None, :], north_wind[:, face_number], north_speed[:, None, :]], -2
        )
        speed_faces.append(0.5 * (speeds[:, :-1, :] + speeds[:, 1:, :]))
    return (jnp.stack(padded_faces, 2), jnp.stack(speed_faces, 1), row_wind)


def regrid(tracer, tile_source, tile_target, intersection, band_count):
    scenarios = tracer.shape[0]
    levels = tracer.shape[1]
    batch_rows = scenarios * levels
    block_cells = intersection.shape[1]
    blocks = tracer.astype(jnp.bfloat16).reshape(batch_rows, -1, block_cells)
    chosen = jnp.take(blocks, tile_source, axis=1)
    partial_value = jnp.einsum(
        "btk,tkc->tbc", chosen, intersection, preferred_element_type=jnp.float32
    )
    target_band = tile_target // TGT_DEV
    target_block = tile_target % TGT_DEV
    band_hot = (target_band[:, None] == jnp.arange(band_count)[None, :]).astype(jnp.int32)
    rank = jnp.sum((jnp.cumsum(band_hot, 0) - band_hot) * band_hot, 1)
    slot = jnp.where(rank < SLOTS, target_band * SLOTS + rank, -1)
    slot_hot = (slot[None, :] == jnp.arange(band_count * SLOTS)[:, None]).astype(jnp.float32)
    slotted = jnp.einsum(
        "st,tbc->sbc", slot_hot, partial_value, precision=lax.Precision.HIGHEST
    )
    slot_block = jnp.sum(slot_hot * target_block[None, :].astype(jnp.float32), 1)
    index_rows = jnp.zeros((band_count, 8, block_cells), jnp.float32)
    index_rows = index_rows.at[:, 0, :SLOTS].set(slot_block.reshape(band_count, SLOTS))
    send = jnp.concatenate(
        [slotted.reshape(band_count, SLOTS * batch_rows, block_cells), index_rows], 1
    )
    got = lax.all_to_all(send, "space", 0, 0, tiled=True)
    values = got[:, : SLOTS * batch_rows].reshape(band_count * SLOTS, batch_rows, block_cells)
    got_block = got[:, SLOTS * batch_rows, :SLOTS].reshape(-1)
    block_hot = (got_block[None, :] == jnp.arange(TGT_DEV)[:, None].astype(jnp.float32)).astype(
        jnp.float32
    )
    summed = jnp.einsum("ks,sbc->bkc", block_hot, values, precision=lax.Precision.HIGHEST)
    return summed.reshape(scenarios, levels, TGT_DEV, block_cells)


def local(concentration, emissions, courant, tile_source, tile_target, intersection):
    band_count = lax.axis_size("space")
    position = lax.axis_index("space")
    tracer = concentration.at[:, 0].add(emissions)
    east_wind = courant[0]
    north_wind = courant[1]
    edge_wind = None
    row_wind = None
    for step_number in range(2):
        padded, courant_faces, edge_wind = column_halos(
            tracer, east_wind, north_wind, position, band_count, edge_wind
        )
        tracer = parabola_sweep(padded, courant_faces, 4)
        padded, courant_faces, row_wind = row_halos(
            tracer, east_wind, north_wind, position, band_count, row_wind
        )
        tracer = parabola_sweep(padded, courant_faces, 3)
    regridded = regrid(tracer, tile_source, tile_target, intersection, band_count)
    scenarios = tracer.shape[0]
    everyone = lax.all_gather(regridded, "scen", axis=0, tiled=True)
    moment_sums = jnp.stack([jnp.sum(everyone, 0), jnp.sum(everyone * everyone, 0)])
    ensemble_moments = moment_sums / (scenarios * lax.axis_size("scen"))
    return (tracer, regridded, ensemble_moments)


def solution(mesh):
    return jax.shard_map(
        local,
        mesh=mesh,
        in_specs=(
            P("scen", None, None, "space", None),
            P("scen", None, "space", None),
            P(None, None, None, "space", None),
            P("space"),
            P("space"),
            P("space", None, None),
        ),
        out_specs=(
            P("scen", None, None, "space", None),
            P("scen", None, "space", None),
            P(None, None, "space", None),
        ),
        check_vma=False,
    )
```

time: 1000 us -> 341 us (0.34)
  waiting for transfers between devices: 692 us -> 110 us
  blocking collectives: 91.1 us -> 0 us
  starting transfers between devices: 5.47 us -> 54.6 us
  other arithmetic: 78.5 us -> 36.2 us
    psum x3 -> x0, waiting for transfers between devices: 593 us -> none  [the longest x2 516 us: broadcast(): return lax.psum(kept, axis)]
    reduce_scatter x1 -> x0, waiting for transfers between devices: 99.2 us -> none  [local(): lax.psum_scatter(empty.at[slot_index].add(partial_value, mode='drop'), 's...]
    all_gather x2 -> x0, blocking collectives: 91.1 us -> none  [row_halos(): lax.all_gather(jnp.concatenate([columns, column_speed], 0), 'space', axis...]
    all_to_all x0 -> x5, waiting for transfers between devices: none -> 67.4 us  [the longest x1 52 us: regrid(): got = lax.all_to_all(send, 'space', 0, 0, tiled=True)]
    all_to_all x0 -> x5, starting transfers between devices: none -> 51.7 us  [the longest x2 27.2 us: edge_rows(): got = lax.all_to_all(send, 'space', 0, 0, tiled=True)]
    all_gather x0 -> x1, waiting for transfers between devices: none -> 42.5 us  [local(): everyone = lax.all_gather(regridded, 'scen', axis=0, tiled=True)]
    slice x48 -> x24, local copies, waits for them, and re-layouts: 38.2 us -> 8.64 us  [the longest x2 1.9 us: row_halos(): packed[:layer_rows]]
    scatter-add x1 -> x0, other arithmetic: 27.1 us -> none  [local(): empty.at[slot_index].add(partial_value, mode='drop')]
  transfers between devices with their start and end apart: 8 -> 10, of which waited for: 4 -> 4; matrix products, arithmetic and copies ran while one was open for 7% -> 13% of each run, Pallas kernels for 0% -> 0%
where the time goes in v1:
time: 341 us; the launch traced here: 335 us
  local copies, waits for them, and re-layouts  110 us (32%)
  waiting for transfers between devices  110 us (32%)
  starting transfers between devices  54.6 us (16%)
  other arithmetic  36.2 us (11%)
  between operations  16.3 us (5%)
  matrix products  8.66 us (3%)
    all_to_all x1, waiting for transfers between devices, regrid(): got = lax.all_to_all(send, 'space', 0, 0, tiled=True)  52 us
    all_gather x1, waiting for transfers between devices, local(): everyone = lax.all_gather(regridded, 'scen', axis=0, tiled=True)  42.5 us
    all_to_all x2, starting transfers between devices, edge_rows(): got = lax.all_to_all(send, 'space', 0, 0, tiled=True)  27.2 us
    all_to_all x2, starting transfers between devices, edge_columns(): got = lax.all_to_all(send, 'space', 0, 0, tiled=True)  15 us
    unnamed x40, other arithmetic  10.3 us
    all_to_all x1, starting transfers between devices, regrid(): got = lax.all_to_all(send, 'space', 0, 0, tiled=True)  9.54 us
    reshape x4, local copies, waits for them, and re-layouts, by_destination(): values.reshape(values.shape[:-1] + (band_count, width // band_count))  8.99 us
    rev x10, local copies, waits for them, and re-layouts, by_destination(): return jnp.flip(jnp.moveaxis(blocks, -2, 0), 0).reshape(band_count, -1)  8.87 us
  transfers between devices with their start and end apart: 10, of which 4 were waited for; matrix products, arithmetic and copies ran while one was open for 13% of the time, Pallas kernels for 0%

profile of v1, /device:TPU:2, one launch (start us, length us, event | category | flops | bytes accessed | tf_op | source)
XLA Modules:
  0.0 335.2 jit_solution(12581908648371963601)
XLA Ops:
  23.3 12.2 %all-to-all-start = ((f32[32,1,1152]{2,1,0:T(1,128)}), f32[32,1,1152]{2,1,0:T(1,128)S(1)}, u32[]{:S(2)}, u32[]{:S(2)}) async-start(f32[32,1,1152]{2,1,0:T(1,128)} %copy.508), calls=%async_computation | async-start | bytes 294912 | tf_op jit(solution)/shard_map/all_to_all | solution.py:87
  71.3 1.8 copy.527
  74.1 1.8 copy.525
  78.9 1.7 copy.530
  80.7 9.8 %all-to-all-start.1 = ((f32[32,1,1152]{2,1,0:T(1,128)}), f32[32,1,1152]{2,1,0:T(1,128)}, u32[]{:S(2)}, u32[]{:S(2)}) async-start(f32[32,1,1152]{2,1,0:T(1,128)} %copy.530), calls=%async_computation.1 | async-start | bytes 294912 | tf_op jit(solution)/shard_map/all_to_all | solution.py:140
  90.5 1.7 copy.521
  92.2 1.8 reshape.3064
  94.0 1.7 copy.534
  95.7 1.8 reshape.3072
  97.5 1.7 pad_maximum_fusion.1
  99.3 1.7 pad_maximum_fusion
  107.0 2.1 reshape.3108
  112.2 1.6 rev.144
  113.8 2.2 rev.143
  132.7 3.2 reshape.3080
  135.9 3.0 rev.149
  138.9 3.2 reshape.3079
  142.1 3.0 rev.148
  146.5 2.3 copy.573
  148.8 1.8 copy.574
  150.6 14.9 %all-to-all-start.2 = ((f32[32,1,864]{2,1,0:T(1,128)}), f32[32,1,864]{2,1,0:T(1,128)}, u32[]{:S(2)}, u32[]{:S(2)}) async-start(f32[32,1,864]{2,1,0:T(1,128)} %copy.574), calls=%async_computation.2 | async-start | bytes 229376 | tf_op jit(solution)/shard_map/all_to_all | solution.py:87
  166.3 8.3 %all-to-all-done.2 = f32[32,1,864]{2,1,0:T(1,128)} async-done(((f32[32,1,864]{2,1,0:T(1,128)}), f32[32,1,864]{2,1,0:T(1,128)}, u32[]{:S(2)}, u32[]{:S(2)}) %all-to-all-start.2) | async-done | bytes 110624 | tf_op jit(solution)/shard_map/all_to_all | solution.py:87
  186.1 5.2 %all-to-all-start.3 = ((f32[32,1,864]{2,1,0:T(1,128)}), f32[32,1,864]{2,1,0:T(1,128)S(1)}, u32[]{:S(2)}, u32[]{:S(2)}) async-start(f32[32,1,864]{2,1,0:T(1,128)} %copy.587), calls=%async_computation.3 | async-start | bytes 229376 | tf_op jit(solution)/shard_map/all_to_all | solution.py:140
  191.9 2.0 collective-permute-start.3
  193.9 7.0 %all-to-all-done.3 = f32[32,1,864]{2,1,0:T(1,128)S(1)} async-done(((f32[32,1,864]{2,1,0:T(1,128)}), f32[32,1,864]{2,1,0:T(1,128)S(1)}, u32[]{:S(2)}, u32[]{:S(2)}) %all-to-all-start.3) | async-done | bytes 110624 | tf_op jit(solution)/shard_map/all_to_all | solution.py:140
  208.2 1.8 gather_fusion
  210.0 4.9 %fusion.62 = f32[270,8,128]{2,1,0:T(8,128)S(1)} fusion(bf16[270,128,128]{2,1,0:T(8,128)(2,1)} %param.23, bf16[270,8,128]{2,1,0:T(8,128)(2,1)S(1)} %gather_fusion, pred[270]{0:T(512)(128)(4,1)S(1)} %copy-done.61), kind=kOutput, calls=%fused_computation.103 | convolution fusion | flops 71055360 | bytes 10506510 | tf_op jit(solution)/shard_map/btk,tkc->tbc/dot_general | solution.py:229
  214.9 2.0 fusion.28
  219.7 9.5 %all-to-all-start.4 = ((f32[32,136,128]{2,1,0:T(8,128)}), f32[32,136,128]{2,1,0:T(8,128)S(1)}, u32[]{:S(2)}, u32[]{:S(2)}) async-start(f32[32,136,128]{2,1,0:T(8,128)} %select_maximum_fusion), calls=%async_computation.4 | async-start | bytes 4456448 | tf_op jit(solution)/shard_map/all_to_all | solution.py:247
  229.3 52.0 %all-to-all-done.4 = f32[32,136,128]{2,1,0:T(8,128)S(1)} async-done(((f32[32,136,128]{2,1,0:T(8,128)}), f32[32,136,128]{2,1,0:T(8,128)S(1)}, u32[]{:S(2)}, u32[]{:S(2)}) %all-to-all-start.4) | async-done | bytes 2228256 | tf_op jit(solution)/shard_map/all_to_all | solution.py:247
  281.8 1.7 fusion
  283.5 42.5 %all-gather.3.cloned.1.call-done = f32[64,32,128]{2,1,0:T(8,128)} async-done(((f32[8,32,128]{2,1,0:T(8,128)}), f32[64,32,128]{2,1,0:T(8,128)}) %all-gather.3.cloned.1.call-update) | async-done | bytes 1048592 | tf_op jit(solution)/shard_map/all_gather | solution.py:276
  (416 shorter events, 106.7 us)
Async XLA Ops:
  21.1 14.4 %copy-start.60 = (s32[270]{0:T(512)S(1)}, s32[270]{0:T(512)}, u32[]{:S(2)}) copy-start(s32[270]{0:T(512)} %param.21) | copy-start | bytes 3244
  23.3 22.4 %all-to-all-start = ((f32[32,1,1152]{2,1,0:T(1,128)}), f32[32,1,1152]{2,1,0:T(1,128)S(1)}, u32[]{:S(2)}, u32[]{:S(2)}) async-start(f32[32,1,1152]{2,1,0:T(1,128)} %copy.508), calls=%async_computation | async-start | bytes 294912 | tf_op jit(solution)/shard_map/all_to_all | solution.py:87
  58.7 5.9 %copy-start.16 = (f32[1,8,12,384]{3,1,2,0:T(8,128)S(1)}, f32[1,8,12,384]{3,1,2,0:T(8,128)}, u32[]{:S(2)}) copy-start(f32[1,8,12,384]{3,1,2,0:T(8,128)} %get-tuple-element.157) | copy-start | bytes 442372
  60.9 3.3 copy-start.35
  60.9 3.4 %copy-start.43 = (f32[1,8,12,3]{3,1,2,0:T(8,128)S(1)}, f32[1,8,12,3]{3,1,2,0:T(8,128)}, u32[]{:S(2)}) copy-start(f32[1,8,12,3]{3,1,2,0:T(8,128)} %copy.512) | copy-start | bytes 3460
  60.9 3.5 %copy-start.17 = (f32[1,8,12,384]{3,1,2,0:T(8,128)S(1)}, f32[1,8,12,384]{3,1,2,0:T(8,128)}, u32[]{:S(2)}) copy-start(f32[1,8,12,384]{3,1,2,0:T(8,128)} %get-tuple-element.158) | copy-start | bytes 442372
  60.9 3.5 %copy-start.34 = (f32[1,8,12,3]{3,1,2,0:T(8,128)S(1)}, f32[1,8,12,3]{3,1,2,0:T(8,128)}, u32[]{:S(2)}) copy-start(f32[1,8,12,3]{3,1,2,0:T(8,128)} %get-tuple-element.152) | copy-start | bytes 3460
  60.9 3.5 %copy-start.44 = (f32[1,8,12,3]{3,1,2,0:T(8,128)S(1)}, f32[1,8,12,3]{3,1,2,0:T(8,128)}, u32[]{:S(2)}) copy-start(f32[1,8,12,3]{3,1,2,0:T(8,128)} %copy.513) | copy-start | bytes 3460
  60.9 3.6 %copy-start.33 = (f32[1,8,12,3]{3,1,2,0:T(8,128)S(1)}, f32[1,8,12,3]{3,1,2,0:T(8,128)}, u32[]{:S(2)}) copy-start(f32[1,8,12,3]{3,1,2,0:T(8,128)} %get-tuple-element.151) | copy-start | bytes 3460
  60.9 3.6 %copy-start.42 = (f32[1,8,12,3]{3,1,2,0:T(8,128)S(1)}, f32[1,8,12,3]{3,1,2,0:T(8,128)}, u32[]{:S(2)}) copy-start(f32[1,8,12,3]{3,1,2,0:T(8,128)} %copy.514) | copy-start | bytes 3460
  69.7 4.3 %copy-start.59 = (f32[288]{0:T(512)S(1)}, f32[288]{0:T(512)}, u32[]{:S(2)}) copy-start(f32[288]{0:T(512)} %reshape_squeeze.21) | copy-start | bytes 3460
  69.7 7.0 %copy-start.58 = (f32[288]{0:T(512)S(1)}, f32[288]{0:T(512)}, u32[]{:S(2)}) copy-start(f32[288]{0:T(512)} %reshape_squeeze.20) | copy-start | bytes 3460
  80.7 21.8 %all-to-all-start.1 = ((f32[32,1,1152]{2,1,0:T(1,128)}), f32[32,1,1152]{2,1,0:T(1,128)}, u32[]{:S(2)}, u32[]{:S(2)}) async-start(f32[32,1,1152]{2,1,0:T(1,128)} %copy.530), calls=%async_computation.1 | async-start | bytes 294912 | tf_op jit(solution)/shard_map/all_to_all | solution.py:140
  99.2 18.3 %collective-permute-start.1 = (f32[192,384]{1,0:T(8,128)}, f32[192,384]{1,0:T(8,128)}, u32[]{:S(2)}, u32[]{:S(2)}) collective-permute-start(f32[192,384]{1,0:T(8,128)} %pad_maximum_fusion.1), channel_id=1, source_target_pairs={{8,0},{16,8},{24,16},{32,24},{40,32},{48,40},{56,48},{64,56},{72,6... | collective-permute-start | bytes 884744 | tf_op jit(solution)/shard_map/ppermute | solution.py:13
  101.0 18.0 %collective-permute-start = (f32[192,384]{1,0:T(8,128)}, f32[192,384]{1,0:T(8,128)}, u32[]{:S(2)}, u32[]{:S(2)}) collective-permute-start(f32[192,384]{1,0:T(8,128)} %pad_maximum_fusion), channel_id=1, source_target_pairs={{248,0},{0,8},{8,16},{16,24},{24,32},{32,40},{40,48},{48,56},{56,6... | collective-permute-start | bytes 884744 | tf_op jit(solution)/shard_map/ppermute | solution.py:13
  109.9 6.1 %copy-start.41 = (f32[1,8,3,384]{3,2,1,0:T(4,128)S(1)}, f32[1,8,3,384]{3,2,1,0:T(4,128)}, u32[]{:S(2)}) copy-start(f32[1,8,3,384]{3,2,1,0:T(4,128)} %get-tuple-element.196) | copy-start | bytes 110596
  110.0 11.3 %copy-start.9 = (f32[8,1,12,384]{3,0,2,1:T(8,128)S(1)}, f32[8,1,12,384]{3,0,2,1:T(8,128)}, u32[]{:S(2)}) copy-start(f32[8,1,12,384]{3,0,2,1:T(8,128)} %get-tuple-element.124) | copy-start | bytes 442372
  150.6 24.1 %all-to-all-start.2 = ((f32[32,1,864]{2,1,0:T(1,128)}), f32[32,1,864]{2,1,0:T(1,128)}, u32[]{:S(2)}, u32[]{:S(2)}) async-start(f32[32,1,864]{2,1,0:T(1,128)} %copy.574), calls=%async_computation.2 | async-start | bytes 229376 | tf_op jit(solution)/shard_map/all_to_all | solution.py:87
  166.3 13.1 %copy-start.21 = (f32[1,8,12,384]{3,1,2,0:T(8,128)S(1)}, f32[1,8,12,384]{3,1,2,0:T(8,128)}, u32[]{:S(2)}) copy-start(f32[1,8,12,384]{3,1,2,0:T(8,128)} %get-tuple-element.115) | copy-start | bytes 442372
  166.3 13.1 %copy-start.40 = (f32[1,8,12,3]{3,1,2,0:T(8,128)S(1)}, f32[1,8,12,3]{3,1,2,0:T(8,128)}, u32[]{:S(2)}) copy-start(f32[1,8,12,3]{3,1,2,0:T(8,128)} %get-tuple-element.109) | copy-start | bytes 3460
  166.3 13.3 %copy-start.20 = (f32[1,8,12,384]{3,1,2,0:T(8,128)S(1)}, f32[1,8,12,384]{3,1,2,0:T(8,128)}, u32[]{:S(2)}) copy-start(f32[1,8,12,384]{3,1,2,0:T(8,128)} %get-tuple-element.114) | copy-start | bytes 442372
  166.3 13.3 %copy-start.39 = (f32[1,8,12,3]{3,1,2,0:T(8,128)S(1)}, f32[1,8,12,3]{3,1,2,0:T(8,128)}, u32[]{:S(2)}) copy-start(f32[1,8,12,3]{3,1,2,0:T(8,128)} %get-tuple-element.108) | copy-start | bytes 3460
  166.3 14.2 %copy-start.19 = (f32[1,8,12,384]{3,1,2,0:T(8,128)S(1)}, f32[1,8,12,384]{3,1,2,0:T(8,128)}, u32[]{:S(2)}) copy-start(f32[1,8,12,384]{3,1,2,0:T(8,128)} %get-tuple-element.113) | copy-start | bytes 442372
  166.3 14.2 %copy-start.38 = (f32[1,8,12,3]{3,1,2,0:T(8,128)S(1)}, f32[1,8,12,3]{3,1,2,0:T(8,128)}, u32[]{:S(2)}) copy-start(f32[1,8,12,3]{3,1,2,0:T(8,128)} %get-tuple-element.107) | copy-start | bytes 3460
  175.9 4.7 %copy-start.37 = (f32[1,8,12,3]{3,1,2,0:T(8,128)S(1)}, f32[1,8,12,3]{3,1,2,0:T(8,128)}, u32[]{:S(2)}) copy-start(f32[1,8,12,3]{3,1,2,0:T(8,128)} %get-tuple-element.106) | copy-start | bytes 3460
  177.4 3.4 %copy-start.36 = (f32[1,8,12,3]{3,1,2,0:T(8,128)S(1)}, f32[1,8,12,3]{3,1,2,0:T(8,128)}, u32[]{:S(2)}) copy-start(f32[1,8,12,3]{3,1,2,0:T(8,128)} %get-tuple-element.105) | copy-start | bytes 3460
  186.1 14.8 %all-to-all-start.3 = ((f32[32,1,864]{2,1,0:T(1,128)}), f32[32,1,864]{2,1,0:T(1,128)S(1)}, u32[]{:S(2)}, u32[]{:S(2)}) async-start(f32[32,1,864]{2,1,0:T(1,128)} %copy.587), calls=%async_computation.3 | async-start | bytes 229376 | tf_op jit(solution)/shard_map/all_to_all | solution.py:140
  191.5 12.7 %collective-permute-start.2 = (f32[144,384]{1,0:T(8,128)S(1)}, f32[144,384]{1,0:T(8,128)S(1)}, u32[]{:S(2)}, u32[]{:S(2)}) collective-permute-start(f32[144,384]{1,0:T(8,128)S(1)} %reshape.3081), channel_id=1, source_target_pairs={{248,0},{0,8},{8,16},{16,24},{24,32},{32,40},{40,48},{48,56},{56,6... | collective-permute-start | bytes 663560 | tf_op jit(solution)/shard_map/ppermute | solution.py:13
  191.9 12.5 %collective-permute-start.3 = (f32[144,384]{1,0:T(8,128)S(1)}, f32[144,384]{1,0:T(8,128)S(1)}, u32[]{:S(2)}, u32[]{:S(2)}) collective-permute-start(f32[144,384]{1,0:T(8,128)S(1)} %reshape.3086), channel_id=1, source_target_pairs={{8,0},{16,8},{24,16},{32,24},{40,32},{48,40},{56,48},{64,56},{72,6... | collective-permute-start | bytes 663560 | tf_op jit(solution)/shard_map/ppermute | solution.py:13
  210.0 4.9 %copy-start.56 = (s32[270]{0:T(512)S(1)}, s32[270]{0:T(512)}, u32[]{:S(2)}) copy-start(s32[270]{0:T(512)} %copy-done.55) | copy-start | bytes 3244
  219.7 61.6 %all-to-all-start.4 = ((f32[32,136,128]{2,1,0:T(8,128)}), f32[32,136,128]{2,1,0:T(8,128)S(1)}, u32[]{:S(2)}, u32[]{:S(2)}) async-start(f32[32,136,128]{2,1,0:T(8,128)} %select_maximum_fusion), calls=%async_computation.4 | async-start | bytes 4456448 | tf_op jit(solution)/shard_map/all_to_all | solution.py:247
  229.3 96.7 %all-gather.3.cloned.1.call-start = ((), (), s32[]{:S(2)}) async-start(), calls=%async_computation.5 | async-start | bytes 1179648 | tf_op jit(solution)/shard_map/all_gather | solution.py:276
  (41 other events, 50.6 us)
Sparse Core Ops, SparseCore 0:
  283.6 42.3 all-gather.2
